TPU v7x, 256 devices: a whole 4x4x8 slice. The times are simulated.
256 devices in a mesh: dp: 8 (over y, core), seq: 32 (over x, z).
Axes of the slice: x: 4, y: 4, z: 8, core: 2. Of those that a mesh axis runs over, the one named last changes fastest.
Arguments:
- queries: bfloat16 [16, 2048, 1536], P('dp', 'seq'), may hold values from -6 to 6
- key_rows: bfloat16 [16, 2048, 1536], P('dp', 'seq'), may hold values from -6 to 6
- value_rows: bfloat16 [16, 2048, 1536], P('dp', 'seq'), may hold values from -6 to 6
- layer_input: bfloat16 [16, 2048, 1536], P('dp', 'seq'), may hold values from -6 to 6
- utt_lengths: int32 [16], P('dp'), may hold values from 512 to 2048, as said below
- out_weight: bfloat16 [1536, 1536], replicated, may hold values from -0.15625 to 0.15625
- conv_kernel: bfloat16 [31, 1536], replicated, may hold values from -1 to 1
- conv_cotangent: bfloat16 [16, 2048, 1536], P('dp', 'seq'), may hold values from -6 to 6
- pick_weight: int32 [23592], replicated, may hold values from 0 to 2359295
- pick_kernel: int32 [476], replicated, may hold values from 0 to 47615
Outputs:
- conv_out: bfloat16 [16, 2048, 1536], P('dp', 'seq')
- context_grad: bfloat16 [16, 2048, 1536], P('dp', 'seq')
- weight_picks: float32 [23592], replicated
- kernel_picks: float32 [476], replicated
Inputs may be any that keep to these rules, and one draw needn't show every extreme that they name: `utt_lengths`: the first utterance fills all 2048 slots and the last has 512 valid frames.
All inputs are finite; a program needn't handle non-finite values.
Results may differ from a plain program's by a relative error of at most 0.0056.
Values may be sent and summed in bfloat16 or wider, within the bound.
No kernel may reach another device: no remote copies, remote signals or barrier semaphores. Data moves between devices by JAX's collectives and lax.ppermute only.
A program may use at most 128 MiB of HBM per device.

v0:
```python
import math
import jax
import jax.numpy as jnp
from jax import lax
from jax.sharding import PartitionSpec as P

HEADS = 16
neg_big = -1e30


def padded(value, sides, width):
    for axis, dim in sides:
        count, length = (lax.axis_size(axis), value.shape[dim])
        up = [(i, (i + 1) % count) for i in range(count - 1)]
        down = [(j, i) for i, j in up]
        last = lax.slice_in_dim(value, length - width, length, axis=dim)
        leading = lax.slice_in_dim(value, 0, width, axis=dim)
        before = lax.ppermute(last, axis, up)
        after = lax.ppermute(leading, axis, down)
        value = jnp.concatenate([before, value, after], axis=dim)
    return value


def softmax_rows(scores, key_ok):
    scores = jnp.where(key_ok, scores, neg_big)
    row_max = jnp.max(scores, axis=-1, keepdims=True)
    probs = jnp.exp(scores - row_max)
    return (probs.astype(jnp.bfloat16), jnp.sum(probs, axis=-1))


def pick_entries(table, picks):
    flat = table.reshape(-1)
    lane = math.gcd(flat.shape[0], 128)
    blocks = flat.reshape(flat.shape[0] // lane, lane)
    chosen = jnp.take(blocks, picks // lane, axis=0)
    lane_ids = jnp.arange(lane, dtype=jnp.int32)
    hit = lane_ids[None, :] == (picks % lane)[:, None]
    return jnp.sum(jnp.where(hit, chosen, jnp.float32(0.0)), axis=1)


def on_device(
    queries,
    key_rows,
    value_rows,
    layer_input,
    utt_lengths,
    out_weight,
    conv_kernel,
    conv_cotangent,
    pick_weight,
    pick_kernel,
):
    local_utts, frames_dev, width = queries.shape
    seq_count = lax.axis_size("seq")
    full_frames = frames_dev * seq_count
    head_size = width // HEADS
    score_scale = 1.0 / math.sqrt(head_size)
    first_frame = lax.axis_index("seq") * frames_dev
    local_ids = first_frame + jnp.arange(frames_dev, dtype=jnp.int32)
    valid_rows = (local_ids[None, :] < utt_lengths[:, None]).astype(jnp.float32)
    all_keys, all_values = (
        lax.all_gather(key_rows, "seq", axis=1, tiled=True),
        lax.all_gather(value_rows, "seq", axis=1, tiled=True),
    )
    full_ids = jnp.arange(full_frames, dtype=jnp.int32)

    def one_utt(item):
        query_utt, key_utt, value_utt, length_utt = item
        query_heads = query_utt.reshape(frames_dev, HEADS, head_size)
        key_heads = key_utt.reshape(full_frames, HEADS, head_size)
        value_heads = value_utt.reshape(full_frames, HEADS, head_size)
        scores = (
            jnp.einsum("qhd,khd->hqk", query_heads, key_heads, preferred_element_type=jnp.float32)
            * score_scale
        )
        weights, denom = softmax_rows(scores, (full_ids < length_utt)[None, None, :])
        out_rows = jnp.einsum(
            "hqk,khd->qhd", weights, value_heads, preferred_element_type=jnp.float32
        )
        out_rows = out_rows / denom.transpose(1, 0)[:, :, None]
        return out_rows.astype(jnp.bfloat16).reshape(frames_dev, width)

    context = lax.map(one_utt, (queries, all_keys, all_values, utt_lengths))
    context_flat = context.reshape(local_utts * frames_dev, width)
    projected = jnp.dot(context_flat, out_weight, preferred_element_type=jnp.float32).reshape(
        local_utts, frames_dev, width
    )
    hidden = ((layer_input.astype(jnp.float32) + projected) * valid_rows[:, :, None]).astype(
        jnp.bfloat16
    )
    tap_count = conv_kernel.shape[0]
    half_taps = (tap_count - 1) // 2
    kernel_f = conv_kernel.astype(jnp.float32)
    hidden_pad = padded(hidden, (("seq", 1),), half_taps)
    cot_f = conv_cotangent.astype(jnp.float32)
    conv_sum = jnp.zeros((local_utts, frames_dev, width), jnp.float32)
    kernel_rows = []
    for offset in range(tap_count):
        window = hidden_pad[:, offset : offset + frames_dev].astype(jnp.float32)
        conv_sum = conv_sum + kernel_f[offset] * window
        kernel_rows.append(jnp.sum(window * cot_f, axis=(0, 1)))
    conv_out = conv_sum.astype(jnp.bfloat16)
    kernel_grad = jnp.stack(kernel_rows)
    cot_pad = padded(conv_cotangent, (("seq", 1),), half_taps).astype(jnp.float32)
    back_sum = jnp.zeros((local_utts, frames_dev, width), jnp.float32)
    for offset in range(tap_count):
        begin = 2 * half_taps - offset
        back_sum = back_sum + kernel_f[offset] * cot_pad[:, begin : begin + frames_dev]
    hidden_grad = (back_sum * valid_rows[:, :, None]).astype(jnp.bfloat16)
    grad_flat = hidden_grad.reshape(local_utts * frames_dev, width)
    weight_grad = lax.dot_general(
        context_flat, grad_flat, (((0,), (0,)), ((), ())), preferred_element_type=jnp.float32
    )
    context_grad = lax.dot_general(
        grad_flat, out_weight, (((1,), (1,)), ((), ())), preferred_element_type=jnp.float32
    )
    context_grad = context_grad.reshape(local_utts, frames_dev, width).astype(jnp.bfloat16)
    weight_vals = pick_entries(weight_grad, pick_weight)
    kernel_vals = pick_entries(kernel_grad, pick_kernel)
    weight_sum, kernel_sum = lax.psum((weight_vals, kernel_vals), ("dp", "seq"))
    total_slots = local_utts * lax.axis_size("dp") * full_frames
    norm_factor = 1.0 / math.sqrt(total_slots)
    return (conv_out, context_grad, weight_sum * norm_factor, kernel_sum * norm_factor)


def solution(mesh):
    placed = (
        P("dp", "seq", None),
        P("dp", "seq", None),
        P("dp", "seq", None),
        P("dp", "seq", None),
        P("dp"),
        P(),
        P(),
        P("dp", "seq", None),
        P(),
        P(),
    )
    return jax.shard_map(
        on_device,
        mesh=mesh,
        in_specs=placed,
        out_specs=(P("dp", "seq", None), P("dp", "seq", None), P(), P()),
        check_vma=False,
    )
```

profile of v0, /device:TPU:1, one launch (start us, length us, event | category | flops | bytes accessed | tf_op | source)
XLA Modules:
  0.0 756.6 jit_solution(8033392045944065864)
XLA Ops:
  7.2 2.1 copy.22
  9.4 2.2 copy.23
  12.6 4.4 collective-permute-start.2
  28.5 3.3 fusion.104
  32.1 2.4 fusion.34
  34.5 99.7 %all-gather.3.cloned.1.call-done = bf16[2,2048,1536]{2,0,1:T(2,128)(2,1)} async-done(((bf16[2,64,1536]{2,0,1:T(2,128)(2,1)}), bf16[2,2048,1536]{2,0,1:T(2,128)(2,1)}) %all-gather.3.cloned.1.call-update) | async-done | bytes 12582928 | tf_op jit(solution)/shard_map/all_gather | solution.py:63
  134.2 31.1 %copy.24 = bf16[2,2048,1536]{1,2,0:T(8,128)(2,1)} copy(bf16[2,2048,1536]{2,0,1:T(2,128)(2,1)} %all-gather.3.cloned.1.call-done) | data formatting | bytes 25165824
  165.4 88.2 %all-gather.5.cloned.1.call-done = bf16[2,2048,1536]{2,0,1:T(2,128)(2,1)} async-done(((bf16[2,64,1536]{2,0,1:T(2,128)(2,1)}), bf16[2,2048,1536]{2,0,1:T(2,128)(2,1)}) %all-gather.5.cloned.1.call-update) | async-done | bytes 12582928 | tf_op jit(solution)/shard_map/all_gather | solution.py:62
  253.6 31.1 %copy.25 = bf16[2,2048,1536]{1,2,0:T(8,128)(2,1)} copy(bf16[2,2048,1536]{2,0,1:T(2,128)(2,1)} %all-gather.5.cloned.1.call-done) | data formatting | bytes 25165824
  284.7 51.8 %while.11 = (s32[]{:T(128)}, bf16[2,64,1536]{2,1,0:T(8,128)(2,1)S(1)}, bf16[2,2048,1536]{1,2,0:T(8,128)(2,1)}, s32[2]{0:T(128)S(1)}, bf16[2,64,1536]{2,1,0:T(8,1...) while((s32[]{:T(128)}, bf16[2,64,1536]{2,1,0:T(8,128)(2,1)S(1)}, ...), condition=%wide.region_3.4_spmd.clone, body=%wide.region_0.3_spmd.clone.sunk | while | flops 828571648 | bytes 65302632 | solution.py:83
  284.7 11.9 %constant_dynamic-slice_fusion.5 = (bf16[1,2048,1536]{1,2,0:T(8,128)(2,1)}, bf16[1,2048,1536]{1,2,0:T(8,128)(2,1)}) fusion(bf16[2,2048,1536]{1,2,0:T(8,128)(2,1)} %get-tuple-element.212, s32[]{:T(128)} %get-tuple-element.200, bf16[2,2048,1536]{1,2,0:T(8,128)(2,1)} %get-tuple-element.209), kind=kLoop, calls=%fused_computation.20.clone.1 | loop fusion | bytes 25165828 | tf_op jit(solution)/shard_map/while/body/jit(dynamic_index_in_dim)/dynamic_slice | solution.py:83
  298.2 5.0 fusion.182
  303.2 1.9 fusion.183
  305.1 5.1 fusion.184
  310.6 11.9 %constant_dynamic-slice_fusion.5 = (bf16[1,2048,1536]{1,2,0:T(8,128)(2,1)}, bf16[1,2048,1536]{1,2,0:T(8,128)(2,1)}) fusion(bf16[2,2048,1536]{1,2,0:T(8,128)(2,1)} %get-tuple-element.212, s32[]{:T(128)} %get-tuple-element.200, bf16[2,2048,1536]{1,2,0:T(8,128)(2,1)} %get-tuple-element.209), kind=kLoop, calls=%fused_computation.20.clone.1 | loop fusion | bytes 25165828 | tf_op jit(solution)/shard_map/while/body/jit(dynamic_index_in_dim)/dynamic_slice | solution.py:83
  324.1 5.0 fusion.182
  331.0 5.1 fusion.184
  336.6 5.0 convolution_bitcast_fusion
  342.4 10.5 %reshape_reshape.6 = f32[18432,128]{1,0:T(8,128)} reshape(f32[1536,1536]{1,0:T(8,128)} %convolution_bitcast_fusion) | data formatting | bytes 18874368 | tf_op jit(solution)/shard_map/reshape;reshape | solution.py:34
  353.0 48.0 %gather_fusion = f32[23592,128]{1,0:T(8,128)} fusion(f32[18432,128]{1,0:T(8,128)} %reshape_reshape.6, s32[24576]{0:T(1024)S(1)} %pad_clamp_fusion), kind=kCustom, calls=%fused_computation | custom fusion | bytes 24252576 | tf_op jit(solution)/shard_map/jit(_take)/gather | solution.py:35
  401.3 22.9 %select_reduce_fusion = f32[23592]{0:T(1024)} fusion(f32[23592,128]{1,0:T(8,128)} %gather_fusion, s32[23592]{0:T(1024)S(1)} %copy-done.2, pred[23592]{0:T(1024)(128)(4,1)S(1)} %copy-done.4), kind=kLoop, calls=%fused_computation.25 | loop fusion | flops 12055512 | bytes 12291432 | tf_op jit(solution)/shard_map/reduce_sum | solution.py:38
  427.0 235.6 %all-reduce.2.cloned.1.call-done = f32[23592]{0:T(1024)} async-done(((f32[23592]{0:T(1024)}), f32[23592]{0:T(1024)}) %all-reduce.2.cloned.1.call-update) | async-done | bytes 94384 | tf_op jit(solution)/shard_map/psum | solution.py:120
  670.6 74.1 %psum.15 = f32[476]{0:T(512)S(1)} all-reduce(f32[476]{0:T(512)S(1)} %select_reduce_fusion.1), channel_id=1, replica_groups=mesh['dp'=8,'seq'=32] {'dp','seq'}, use_global_device_ids=true, to_apply=%region_38.39 | all-reduce | flops 476 | bytes 3808 | tf_op jit(solution)/shard_map/psum | solution.py:120
  745.6 4.5 fusion.70
  (237 shorter events, 30.2 us)
Async XLA Ops:
  7.2 127.1 %all-gather.3.cloned.1.call-start = ((), (), s32[]{:S(2)}) async-start(), calls=%async_computation | async-start | bytes 12976128 | tf_op jit(solution)/shard_map/all_gather | solution.py:63
  9.4 244.2 %all-gather.5.cloned.1.call-start = ((), (), s32[]{:S(2)}) async-start(), calls=%async_computation.1 | async-start | bytes 12976128 | tf_op jit(solution)/shard_map/all_gather | solution.py:62
  11.6 650.9 %all-reduce.2.cloned.1.call-start = ((), (), s32[]{:S(2)}) async-start(), calls=%async_computation.2 | async-start | bytes 196608 | tf_op jit(solution)/shard_map/psum | solution.py:120
  12.6 14.5 %collective-permute-start.2 = (bf16[2,15,1536]{2,1,0:T(8,128)(2,1)S(1)}, bf16[2,15,1536]{2,1,0:T(8,128)(2,1)S(1)}, u32[]{:S(2)}, u32[]{:S(2)}) collective-permute-start(bf16[2,15,1536]{2,1,0:T(8,128)(2,1)S(1)} %get-tuple-element.144), channel_id=1, source_target_pairs={{0,1},{1,2},{2,3},{3,4},{4,5},{5,6},{6,7},{7,8},{8,9},{9,10},{10,1... | collective-permute-start | bytes 276488 | tf_op jit(solution)/shard_map/ppermute | solution.py:18
  17.0 10.1 %collective-permute-start.3 = (bf16[2,15,1536]{2,1,0:T(8,128)(2,1)S(1)}, bf16[2,15,1536]{2,1,0:T(8,128)(2,1)S(1)}, u32[]{:S(2)}, u32[]{:S(2)}) collective-permute-start(bf16[2,15,1536]{2,1,0:T(8,128)(2,1)S(1)} %get-tuple-element.145), channel_id=1, source_target_pairs={{1,0},{2,1},{3,2},{4,3},{5,4},{6,5},{7,6},{8,7},{9,8},{10,9},{11,1... | collective-permute-start | bytes 276488 | tf_op jit(solution)/shard_map/ppermute | solution.py:19
  401.0 344.3 %copy-start.6 = (f32[1536]{0:T(1024)S(1)}, f32[1536]{0:T(1024)}, u32[]{:S(2)}) copy-start(f32[1536]{0:T(1024)} %copy-done.5) | copy-start | bytes 18436
  401.0 344.3 %copy-start.8 = (f32[1536]{0:T(1024)S(1)}, f32[1536]{0:T(1024)}, u32[]{:S(2)}) copy-start(f32[1536]{0:T(1024)} %copy-done.7) | copy-start | bytes 18436
  401.0 344.3 %copy-start.10 = (f32[1536]{0:T(1024)S(1)}, f32[1536]{0:T(1024)}, u32[]{:S(2)}) copy-start(f32[1536]{0:T(1024)} %copy-done.9) | copy-start | bytes 18436
  401.0 344.3 %copy-start.12 = (f32[1536]{0:T(1024)S(1)}, f32[1536]{0:T(1024)}, u32[]{:S(2)}) copy-start(f32[1536]{0:T(1024)} %copy-done.11) | copy-start | bytes 18436
  401.0 344.3 %copy-start.14 = (f32[1536]{0:T(1024)S(1)}, f32[1536]{0:T(1024)}, u32[]{:S(2)}) copy-start(f32[1536]{0:T(1024)} %copy-done.13) | copy-start | bytes 18436
  401.0 344.3 %copy-start.16 = (f32[1536]{0:T(1024)S(1)}, f32[1536]{0:T(1024)}, u32[]{:S(2)}) copy-start(f32[1536]{0:T(1024)} %copy-done.15) | copy-start | bytes 18436
  401.0 344.3 %copy-start.18 = (f32[1536]{0:T(1024)S(1)}, f32[1536]{0:T(1024)}, u32[]{:S(2)}) copy-start(f32[1536]{0:T(1024)} %copy-done.17) | copy-start | bytes 18436
  401.0 344.3 %copy-start.20 = (f32[1536]{0:T(1024)S(1)}, f32[1536]{0:T(1024)}, u32[]{:S(2)}) copy-start(f32[1536]{0:T(1024)} %copy-done.19) | copy-start | bytes 18436
  401.1 344.3 %copy-start.22 = (f32[1536]{0:T(1024)S(1)}, f32[1536]{0:T(1024)}, u32[]{:S(2)}) copy-start(f32[1536]{0:T(1024)} %copy-done.21) | copy-start | bytes 18436
  401.1 344.3 %copy-start.24 = (f32[1536]{0:T(1024)S(1)}, f32[1536]{0:T(1024)}, u32[]{:S(2)}) copy-start(f32[1536]{0:T(1024)} %copy-done.23) | copy-start | bytes 18436
  401.1 344.3 %copy-start.26 = (f32[1536]{0:T(1024)S(1)}, f32[1536]{0:T(1024)}, u32[]{:S(2)}) copy-start(f32[1536]{0:T(1024)} %copy-done.25) | copy-start | bytes 18436
  401.1 344.3 %copy-start.28 = (f32[1536]{0:T(1024)S(1)}, f32[1536]{0:T(1024)}, u32[]{:S(2)}) copy-start(f32[1536]{0:T(1024)} %copy-done.27) | copy-start | bytes 18436
  401.1 344.3 %copy-start.30 = (f32[1536]{0:T(1024)S(1)}, f32[1536]{0:T(1024)}, u32[]{:S(2)}) copy-start(f32[1536]{0:T(1024)} %copy-done.29) | copy-start | bytes 18436
  401.1 344.3 %copy-start.32 = (f32[1536]{0:T(1024)S(1)}, f32[1536]{0:T(1024)}, u32[]{:S(2)}) copy-start(f32[1536]{0:T(1024)} %copy-done.31) | copy-start | bytes 18436
  401.1 344.3 %copy-start.34 = (f32[1536]{0:T(1024)S(1)}, f32[1536]{0:T(1024)}, u32[]{:S(2)}) copy-start(f32[1536]{0:T(1024)} %copy-done.33) | copy-start | bytes 18436
  401.1 344.3 %copy-start.36 = (f32[1536]{0:T(1024)S(1)}, f32[1536]{0:T(1024)}, u32[]{:S(2)}) copy-start(f32[1536]{0:T(1024)} %copy-done.35) | copy-start | bytes 18436
  401.1 344.3 %copy-start.38 = (f32[1536]{0:T(1024)S(1)}, f32[1536]{0:T(1024)}, u32[]{:S(2)}) copy-start(f32[1536]{0:T(1024)} %copy-done.37) | copy-start | bytes 18436
  424.3 239.8 %collective-permute-start = (bf16[2,15,1536]{2,1,0:T(8,128)(2,1)S(1)}, bf16[2,15,1536]{2,1,0:T(8,128)(2,1)S(1)}, u32[]{:S(2)}, u32[]{:S(2)}) collective-permute-start(bf16[2,15,1536]{2,1,0:T(8,128)(2,1)S(1)} %get-tuple-element.146), channel_id=1, source_target_pairs={{0,1},{1,2},{2,3},{3,4},{4,5},{5,6},{6,7},{7,8},{8,9},{9,10},{10,1... | collective-permute-start | bytes 276488 | tf_op jit(solution)/shard_map/ppermute | solution.py:18
  425.7 239.7 %collective-permute-start.1 = (bf16[2,15,1536]{2,1,0:T(8,128)(2,1)S(1)}, bf16[2,15,1536]{2,1,0:T(8,128)(2,1)S(1)}, u32[]{:S(2)}, u32[]{:S(2)}) collective-permute-start(bf16[2,15,1536]{2,1,0:T(8,128)(2,1)S(1)} %get-tuple-element.147), channel_id=1, source_target_pairs={{1,0},{2,1},{3,2},{4,3},{5,4},{6,5},{7,6},{8,7},{9,8},{10,9},{11,1... | collective-permute-start | bytes 276488 | tf_op jit(solution)/shard_map/ppermute | solution.py:19
  (58 other events, 6625.0 us)
Sparse Core Ops, SparseCore 0:
  11.2 123.0 all-gather.2
  136.8 116.7 all-gather.4
  424.3 238.1 all-reduce.1
where the time goes:
time: 759 us; the launch traced here: 757 us
  waiting for transfers between devices  424 us (56%)
  local copies, waits for them, and re-layouts  155 us (20%)
  blocking collectives  74.1 us (10%)
  other arithmetic  51.7 us (7%)
  matrix products  28.4 us (4%)
  between operations  15.2 us (2%)
  starting transfers between devices  8.5 us (1%)
    psum x1, waiting for transfers between devices, on_device(): weight_sum, kernel_sum = lax.psum((weight_vals, kernel_vals), ('dp', 'seq'))  236 us
    all_gather x1, waiting for transfers between devices, on_device(): lax.all_gather(value_rows, 'seq', axis=1, tiled=True)  99.7 us
    all_gather x1, waiting for transfers between devices, on_device(): lax.all_gather(key_rows, 'seq', axis=1, tiled=True)  88.2 us
    psum x1, blocking collectives, on_device(): weight_sum, kernel_sum = lax.psum((weight_vals, kernel_vals), ('dp', 'seq'))  74.1 us
    unnamed x154, local copies, waits for them, and re-layouts  66.9 us
    gather x2, local copies, waits for them, and re-layouts, pick_entries(): chosen = jnp.take(blocks, picks // lane, axis=0)  49.1 us
    dynamic_slice x6, local copies, waits for them, and re-layouts, on_device(): context = lax.map(one_utt, (queries, all_keys, all_values, utt_lengths))  25.1 us
    reduce_sum x2, other arithmetic, pick_entries(): return jnp.sum(jnp.where(hit, chosen, jnp.float32(0.0)), axis=1)  23.2 us
  transfers between devices with their start and end apart: 7, of which 3 were waited for; matrix products, arithmetic and copies ran while one was open for 7% of the time, Pallas kernels for 0%

commit v1 on v0

--- a/solution.py
+++ b/solution.py
@@ -59,7 +59,9 @@
     local_ids = first_frame + jnp.arange(frames_dev, dtype=jnp.int32)
     valid_rows = (local_ids[None, :] < utt_lengths[:, None]).astype(jnp.float32)
     all_keys, all_values = (
-        lax.all_gather(key_rows, "seq", axis=1, tiled=True),
+        jnp.concatenate(
+            lax.all_to_all(jnp.stack([key_rows] * lax.axis_size("seq")), "seq", 0, 0), axis=1
+        ),
         lax.all_gather(value_rows, "seq", axis=1, tiled=True),
     )
     full_ids = jnp.arange(full_frames, dtype=jnp.int32)

time: 759 us -> 926 us (1.22)
  waiting for transfers between devices: 424 us -> 581 us
  starting transfers between devices: 8.5 us -> 22.3 us
    ppermute x2, waiting for transfers between devices: 0.01 us -> 344 us  [padded(): before = lax.ppermute(last, axis, up)]
    all_gather x1, waiting for transfers between devices: 99.7 us -> 0.01 us  [on_device(): lax.all_gather(value_rows, 'seq', axis=1, tiled=True)]
    all_gather x1 -> x0, waiting for transfers between devices: 88.2 us -> none  [on_device(): lax.all_gather(key_rows, 'seq', axis=1, tiled=True)]
    unnamed x154 -> x168, local copies, waits for them, and re-layouts: 66.9 us -> 32.7 us
    dynamic_slice x6 -> x10, local copies, waits for them, and re-layouts: 25.1 us -> 43.4 us  [on_device(): context = lax.map(one_utt, (queries, all_keys, all_values, utt_lengths))]
    all_to_all x0 -> x1, starting transfers between devices: none -> 12.1 us  [on_device(): lax.all_to_all(jnp.stack([key_rows] * lax.axis_size('seq')), 'seq', 0, 0)]
    all_to_all x0 -> x1, local copies, waits for them, and re-layouts: none -> 10.9 us  [on_device(): lax.all_to_all(jnp.stack([key_rows] * lax.axis_size('seq')), 'seq', 0, 0)]
  transfers between devices with their start and end apart: 7 -> 7, of which waited for: 3 -> 2; matrix products, arithmetic and copies ran while one was open for 7% -> 3% of each run, Pallas kernels for 0% -> 0%
where the time goes in v1:
time: 926 us; the launch traced here: 924 us
  waiting for transfers between devices  581 us (63%)
  local copies, waits for them, and re-layouts  156 us (17%)
  blocking collectives  74.1 us (8%)
  other arithmetic  46.4 us (5%)
  matrix products  28.4 us (3%)
  starting transfers between devices  22.3 us (2%)
  between operations  15.6 us (2%)
    ppermute x2, waiting for transfers between devices, padded(): before = lax.ppermute(last, axis, up)  344 us
    psum x1, waiting for transfers between devices, on_device(): weight_sum, kernel_sum = lax.psum((weight_vals, kernel_vals), ('dp', 'seq'))  237 us
    psum x1, blocking collectives, on_device(): weight_sum, kernel_sum = lax.psum((weight_vals, kernel_vals), ('dp', 'seq'))  74.1 us
    gather x2, local copies, waits for them, and re-layouts, pick_entries(): chosen = jnp.take(blocks, picks // lane, axis=0)  49.1 us
    dynamic_slice x10, local copies, waits for them, and re-layouts, on_device(): context = lax.map(one_utt, (queries, all_keys, all_values, utt_lengths))  43.4 us
    unnamed x168, local copies, waits for them, and re-layouts  32.7 us
    reduce_sum x2, other arithmetic, pick_entries(): return jnp.sum(jnp.where(hit, chosen, jnp.float32(0.0)), axis=1)  23.2 us
  transfers between devices with their start and end apart: 7, of which 2 were waited for; matrix products, arithmetic and copies ran while one was open for 3% of the time, Pallas kernels for 0%

profile of v1, /device:TPU:1, one launch (start us, length us, event | category | flops | bytes accessed | tf_op | source)
XLA Modules:
  0.0 923.9 jit_solution(9519200711261834282)
XLA Ops:
  7.2 7.1 stack.131
  14.3 12.1 %all-to-all-start = ((bf16[32,2,64,1536]{3,2,1,0:T(8,128)(2,1)}), bf16[32,2,64,1536]{3,2,1,0:T(8,128)(2,1)}, u32[]{:S(2)}, u32[]{:S(2)}) async-start(bf16[32,2,64,1536]{3,2,1,0:T(8,128)(2,1)} %stack.131), calls=%async_computation | async-start | bytes 25165824 | tf_op jit(solution)/shard_map/all_to_all | solution.py:63
  36.9 343.8 %collective-permute-done.2 = bf16[2,15,1536]{2,1,0:T(8,128)(2,1)S(1)} collective-permute-done((bf16[2,15,1536]{2,1,0:T(8,128)(2,1)S(1)}, bf16[2,15,1536]{2,1,0:T(8,128)(2,1)S(1)}, u32[]{:S(2)}, u32[]{:S(2)}) %collective-permute-start.2) | collective-permute-done | bytes 92192 | tf_op jit(solution)/shard_map/ppermute | solution.py:18
  386.9 10.9 %copy.23 = bf16[32,2,64,1536]{3,2,0,1:T(8,128)(2,1)} copy(bf16[32,2,64,1536]{3,2,1,0:T(8,128)(2,1)} %all-to-all-done) | data formatting | bytes 25165824 | tf_op jit(solution)/shard_map/all_to_all | solution.py:63
  397.8 31.2 %copy.24 = bf16[2,2048,1536]{1,2,0:T(8,128)(2,1)} copy(bf16[2,2048,1536]{2,0,1:T(2,128)(2,1)} %all-gather.2.cloned.1.call-done) | data formatting | bytes 25165824
  429.0 70.1 %while.11 = (s32[]{:T(128)}, bf16[2,64,1536]{2,1,0:T(8,128)(2,1)S(1)}, bf16[2,2048,1536]{1,2,0:T(8,128)(2,1)}, s32[2]{0:T(128)S(1)}, bf16[2,64,1536]{2,1,0:T(8,1...) while((s32[]{:T(128)}, bf16[2,64,1536]{2,1,0:T(8,128)(2,1)S(1)}, ...), condition=%wide.region_3.4_spmd.clone, body=%wide.region_0.3_spmd.clone.sunk | while | flops 828571648 | bytes 77885552 | solution.py:85
  430.3 5.9 constant_dynamic-slice_fusion.7
  436.1 8.7 copy.35
  445.0 5.0 fusion.182
  452.0 6.6 constant_dynamic-slice_fusion.6
  458.5 5.1 fusion.184
  465.3 5.9 constant_dynamic-slice_fusion.7
  471.2 8.7 copy.35
  480.1 5.0 fusion.182
  487.0 6.6 constant_dynamic-slice_fusion.6
  493.6 5.1 fusion.184
  499.2 5.0 convolution_bitcast_fusion
  505.1 10.6 %reshape_reshape.6 = f32[18432,128]{1,0:T(8,128)} reshape(f32[1536,1536]{1,0:T(8,128)} %convolution_bitcast_fusion) | data formatting | bytes 18874368 | tf_op jit(solution)/shard_map/reshape;reshape | solution.py:34
  515.6 48.0 %gather_fusion = f32[23592,128]{1,0:T(8,128)} fusion(f32[18432,128]{1,0:T(8,128)} %reshape_reshape.6, s32[24576]{0:T(1024)S(1)} %copy-done.4), kind=kCustom, calls=%fused_computation | custom fusion | bytes 24252576 | tf_op jit(solution)/shard_map/jit(_take)/gather | solution.py:35
  563.9 22.9 %select_reduce_fusion = f32[23592]{0:T(1024)} fusion(f32[23592,128]{1,0:T(8,128)} %gather_fusion, s32[23592]{0:T(1024)S(1)} %copy-done.3, pred[23592]{0:T(1024)(128)(4,1)S(1)} %copy-done.8), kind=kLoop, calls=%fused_computation.25 | loop fusion | flops 12055512 | bytes 12291432 | tf_op jit(solution)/shard_map/reduce_sum | solution.py:38
  588.2 4.4 collective-permute-start
  592.6 236.9 %all-reduce.2.cloned.1.call-done = f32[23592]{0:T(1024)} async-done(((f32[23592]{0:T(1024)}), f32[23592]{0:T(1024)}) %all-reduce.2.cloned.1.call-update) | async-done | bytes 94384 | tf_op jit(solution)/shard_map/psum | solution.py:122
  837.6 74.1 %psum.15 = f32[476]{0:T(512)S(1)} all-reduce(f32[476]{0:T(512)S(1)} %select_reduce_fusion.1), channel_id=1, replica_groups=mesh['dp'=8,'seq'=32] {'dp','seq'}, use_global_device_ids=true, to_apply=%region_38.39 | all-reduce | flops 476 | bytes 3808 | tf_op jit(solution)/shard_map/psum | solution.py:122
  912.6 4.5 fusion.70
  (256 shorter events, 34.3 us)
Async XLA Ops:
  14.3 372.6 %all-to-all-start = ((bf16[32,2,64,1536]{3,2,1,0:T(8,128)(2,1)}), bf16[32,2,64,1536]{3,2,1,0:T(8,128)(2,1)}, u32[]{:S(2)}, u32[]{:S(2)}) async-start(bf16[32,2,64,1536]{3,2,1,0:T(8,128)(2,1)} %stack.131), calls=%async_computation | async-start | bytes 25165824 | tf_op jit(solution)/shard_map/all_to_all | solution.py:63
  26.4 371.4 %all-gather.2.cloned.1.call-start = ((), (), s32[]{:S(2)}) async-start(), calls=%async_computation.1 | async-start | bytes 12976128 | tf_op jit(solution)/shard_map/all_gather | solution.py:65
  27.7 801.9 %all-reduce.2.cloned.1.call-start = ((), (), s32[]{:S(2)}) async-start(), calls=%async_computation.2 | async-start | bytes 196608 | tf_op jit(solution)/shard_map/psum | solution.py:122
  27.8 352.9 %collective-permute-start.2 = (bf16[2,15,1536]{2,1,0:T(8,128)(2,1)S(1)}, bf16[2,15,1536]{2,1,0:T(8,128)(2,1)S(1)}, u32[]{:S(2)}, u32[]{:S(2)}) collective-permute-start(bf16[2,15,1536]{2,1,0:T(8,128)(2,1)S(1)} %get-tuple-element.148), channel_id=1, source_target_pairs={{0,1},{1,2},{2,3},{3,4},{4,5},{5,6},{6,7},{7,8},{8,9},{9,10},{10,1... | collective-permute-start | bytes 276488 | tf_op jit(solution)/shard_map/ppermute | solution.py:18
  30.8 349.9 %collective-permute-start.3 = (bf16[2,15,1536]{2,1,0:T(8,128)(2,1)S(1)}, bf16[2,15,1536]{2,1,0:T(8,128)(2,1)S(1)}, u32[]{:S(2)}, u32[]{:S(2)}) collective-permute-start(bf16[2,15,1536]{2,1,0:T(8,128)(2,1)S(1)} %get-tuple-element.149), channel_id=1, source_target_pairs={{1,0},{2,1},{3,2},{4,3},{5,4},{6,5},{7,6},{8,7},{9,8},{10,9},{11,1... | collective-permute-start | bytes 276488 | tf_op jit(solution)/shard_map/ppermute | solution.py:19
  32.4 351.8 %copy-start.48 = (f32[1536]{0:T(1024)}, f32[1536]{0:T(1024)S(1)}, u32[]{:S(2)}) copy-start(f32[1536]{0:T(1024)S(1)} %get-tuple-element.118) | copy-start | bytes 18436
  32.4 351.8 %copy-start.50 = (f32[1536]{0:T(1024)}, f32[1536]{0:T(1024)S(1)}, u32[]{:S(2)}) copy-start(f32[1536]{0:T(1024)S(1)} %get-tuple-element.119) | copy-start | bytes 18436
  32.4 351.8 %copy-start.52 = (f32[1536]{0:T(1024)}, f32[1536]{0:T(1024)S(1)}, u32[]{:S(2)}) copy-start(f32[1536]{0:T(1024)S(1)} %get-tuple-element.120) | copy-start | bytes 18436
  32.4 351.8 %copy-start.54 = (f32[1536]{0:T(1024)}, f32[1536]{0:T(1024)S(1)}, u32[]{:S(2)}) copy-start(f32[1536]{0:T(1024)S(1)} %get-tuple-element.121) | copy-start | bytes 18436
  32.4 351.8 %copy-start.56 = (f32[1536]{0:T(1024)}, f32[1536]{0:T(1024)S(1)}, u32[]{:S(2)}) copy-start(f32[1536]{0:T(1024)S(1)} %get-tuple-element.122) | copy-start | bytes 18436
  32.4 351.8 %copy-start.58 = (f32[1536]{0:T(1024)}, f32[1536]{0:T(1024)S(1)}, u32[]{:S(2)}) copy-start(f32[1536]{0:T(1024)S(1)} %get-tuple-element.123) | copy-start | bytes 18436
  32.5 351.8 %copy-start.60 = (f32[1536]{0:T(1024)}, f32[1536]{0:T(1024)S(1)}, u32[]{:S(2)}) copy-start(f32[1536]{0:T(1024)S(1)} %get-tuple-element.124) | copy-start | bytes 18436
  32.5 351.8 %copy-start.62 = (f32[1536]{0:T(1024)}, f32[1536]{0:T(1024)S(1)}, u32[]{:S(2)}) copy-start(f32[1536]{0:T(1024)S(1)} %get-tuple-element.125) | copy-start | bytes 18436
  32.5 351.8 %copy-start.64 = (f32[1536]{0:T(1024)}, f32[1536]{0:T(1024)S(1)}, u32[]{:S(2)}) copy-start(f32[1536]{0:T(1024)S(1)} %get-tuple-element.126) | copy-start | bytes 18436
  32.5 351.8 %copy-start.66 = (f32[1536]{0:T(1024)}, f32[1536]{0:T(1024)S(1)}, u32[]{:S(2)}) copy-start(f32[1536]{0:T(1024)S(1)} %get-tuple-element.127) | copy-start | bytes 18436
  32.5 351.8 %copy-start.68 = (f32[1536]{0:T(1024)}, f32[1536]{0:T(1024)S(1)}, u32[]{:S(2)}) copy-start(f32[1536]{0:T(1024)S(1)} %get-tuple-element.128) | copy-start | bytes 18436
  32.5 351.8 %copy-start.70 = (f32[1536]{0:T(1024)}, f32[1536]{0:T(1024)S(1)}, u32[]{:S(2)}) copy-start(f32[1536]{0:T(1024)S(1)} %get-tuple-element.129) | copy-start | bytes 18436
  32.8 351.5 %copy-start.10 = (f32[1536]{0:T(1024)}, f32[1536]{0:T(1024)S(1)}, u32[]{:S(2)}) copy-start(f32[1536]{0:T(1024)S(1)} %get-tuple-element.99) | copy-start | bytes 18436
  32.9 351.5 %copy-start.12 = (f32[1536]{0:T(1024)}, f32[1536]{0:T(1024)S(1)}, u32[]{:S(2)}) copy-start(f32[1536]{0:T(1024)S(1)} %get-tuple-element.100) | copy-start | bytes 18436
  32.9 351.5 %copy-start.14 = (f32[1536]{0:T(1024)}, f32[1536]{0:T(1024)S(1)}, u32[]{:S(2)}) copy-start(f32[1536]{0:T(1024)S(1)} %get-tuple-element.101) | copy-start | bytes 18436
  32.9 351.5 %copy-start.16 = (f32[1536]{0:T(1024)}, f32[1536]{0:T(1024)S(1)}, u32[]{:S(2)}) copy-start(f32[1536]{0:T(1024)S(1)} %get-tuple-element.102) | copy-start | bytes 18436
  32.9 351.5 %copy-start.18 = (f32[1536]{0:T(1024)}, f32[1536]{0:T(1024)S(1)}, u32[]{:S(2)}) copy-start(f32[1536]{0:T(1024)S(1)} %get-tuple-element.103) | copy-start | bytes 18436
  586.9 244.2 %collective-permute-start.1 = (bf16[2,15,1536]{2,1,0:T(8,128)(2,1)S(1)}, bf16[2,15,1536]{2,1,0:T(8,128)(2,1)S(1)}, u32[]{:S(2)}, u32[]{:S(2)}) collective-permute-start(bf16[2,15,1536]{2,1,0:T(8,128)(2,1)S(1)} %get-tuple-element.151), channel_id=1, source_target_pairs={{1,0},{2,1},{3,2},{4,3},{5,4},{6,5},{7,6},{8,7},{9,8},{10,9},{11,1... | collective-permute-start | bytes 276488 | tf_op jit(solution)/shard_map/ppermute | solution.py:19
  588.2 244.4 %collective-permute-start = (bf16[2,15,1536]{2,1,0:T(8,128)(2,1)S(1)}, bf16[2,15,1536]{2,1,0:T(8,128)(2,1)S(1)}, u32[]{:S(2)}, u32[]{:S(2)}) collective-permute-start(bf16[2,15,1536]{2,1,0:T(8,128)(2,1)S(1)} %get-tuple-element.150), channel_id=1, source_target_pairs={{0,1},{1,2},{2,3},{3,4},{4,5},{5,6},{6,7},{7,8},{8,9},{9,10},{10,1... | collective-permute-start | bytes 276488 | tf_op jit(solution)/shard_map/ppermute | solution.py:18
  (66 other events, 17433.5 us)
Sparse Core Ops, SparseCore 0:
  30.4 342.0 all-gather.1
  587.0 242.4 all-reduce.1
